TPU v7x, 512 devices: a whole 4x8x8 slice. The times are simulated.
512 devices in a mesh: req: 64 (over x, z, core), tp: 8 (over y).
Axes of the slice: x: 4, y: 8, z: 8, core: 2. Of those that a mesh axis runs over, the one named last changes fastest.
Arguments:
- residual_input: bfloat16 [8192, 3584], P('req', 'tp'), may hold values from -6 to 6
- new_token_queries: bfloat16 [8192, 4096], P('req', 'tp'), may hold values from -8 to 8
- new_token_keys: bfloat16 [8192, 2048], P('req', 'tp'), may hold values from -8 to 8
- new_token_values: bfloat16 [8192, 2048], P('req', 'tp'), may hold values from -6 to 6
- key_page_pool: bfloat16 [1536, 16, 2048], P('req', None, 'tp'), may hold values from -6 to 6
- value_page_pool: bfloat16 [1536, 16, 2048], P('req', None, 'tp'), may hold values from -6 to 6
- request_page_table: int32 [128, 64], P('req'), may hold values from -1 to 23, as said below
- page_token_length: int32 [128, 64], P('req'), may hold values from 0 to 16, as said below
- request_token_length: int32 [64, 2], P('req'), may hold values from 1 to 96, 128 in all within a row
- request_adapter: int32 [64, 2], P('req'), may hold values from 0 to 63
- adapter_table_row: int32 [64], replicated, may hold values from 0 to 63, each once
- output_weight: bfloat16 [4096, 3584], P('tp'), may hold values from -0.125 to 0.125
- adapter_down_weight: bfloat16 [64, 16, 4096], P('req', None, 'tp'), may hold values from -0.09375 to 0.09375
- adapter_up_weight: bfloat16 [64, 16, 3584], P('req', None, 'tp'), may hold values from -1.5 to 1.5
- norm_scale_row: float32 [3584], P('tp'), may hold values from 0.25 to 1.75
Outputs:
- hidden_out: bfloat16 [8192, 3584], P('req', 'tp')
Inputs may be any that keep to these rules, and one draw needn't show every extreme that they name: request_page_table[q, o] is a page of the pool of owner o (rows o * 24 to o * 24 + 23 of the pools), or -1; so the 2 requests of one index of req take at most 2 pages from one owner, and in every draw the requests of some index of req each take a page from every owner. Requests may share pages. `page_token_length`: 0 exactly where request_page_table is -1; every used page of a request is full but at most one.
All inputs are finite; a program needn't handle non-finite values.
Results may differ from a plain program's by a relative error of at most 0.015.
Values may be sent and summed in bfloat16 or wider, within the bound.
No kernel may reach another device: no remote copies, remote signals or barrier semaphores. Data moves between devices by JAX's collectives and lax.ppermute only.
A program may use at most 64 MiB of HBM per device.

v0:
```python
import jax
import jax.numpy as jnp
from jax import lax
from jax.sharding import PartitionSpec as P

HEAD_SIZE = 256
epsilon = 1e-06
adapter_scale = 2.0
masked_score = -1e30


def attend(query_rows, new_keys, new_values, gathered_keys, gathered_values, usable, owner_request):
    token_count = query_rows.shape[0]
    kv_heads = new_keys.shape[1] // HEAD_SIZE
    group_size = query_rows.shape[1] // new_keys.shape[1]
    requests_here = gathered_keys.shape[0]
    cached_count = gathered_keys.shape[1]
    query_heads = query_rows.reshape(token_count, kv_heads, group_size, HEAD_SIZE)
    past_keys = gathered_keys.reshape(requests_here, cached_count, kv_heads, HEAD_SIZE)
    past_values = gathered_values.reshape(requests_here * cached_count, kv_heads, HEAD_SIZE)
    fresh_keys = new_keys.reshape(token_count, kv_heads, HEAD_SIZE)
    fresh_values = new_values.reshape(token_count, kv_heads, HEAD_SIZE)
    positions = jnp.arange(token_count, dtype=jnp.int32)
    scaling = HEAD_SIZE ** (-0.5)
    past_scores = (
        jnp.einsum("tgqd,rngd->tgqrn", query_heads, past_keys, preferred_element_type=jnp.float32)
        * scaling
    )
    past_mask = usable[None, :, :] & (
        owner_request[:, None, None] == jnp.arange(requests_here, dtype=jnp.int32)[None, :, None]
    )
    past_scores = jnp.where(past_mask[:, None, None, :, :], past_scores, masked_score)
    past_scores = past_scores.reshape(
        token_count, kv_heads, group_size, requests_here * cached_count
    )
    fresh_scores = (
        jnp.einsum("tgqd,ugd->tgqu", query_heads, fresh_keys, preferred_element_type=jnp.float32)
        * scaling
    )
    fresh_mask = (owner_request[:, None] == owner_request[None, :]) & (
        positions[None, :] <= positions[:, None]
    )
    fresh_scores = jnp.where(fresh_mask[:, None, None, :], fresh_scores, masked_score)
    scores = jnp.concatenate([past_scores, fresh_scores], axis=3)
    highest = jnp.max(scores, axis=3, keepdims=True)
    weights = jnp.exp(scores - highest)
    weights = (weights / jnp.sum(weights, axis=3, keepdims=True)).astype(jnp.bfloat16)
    all_values = jnp.concatenate([past_values, fresh_values], axis=0)
    mixed = jnp.einsum("tgqk,kgd->tgqd", weights, all_values, preferred_element_type=jnp.float32)
    return mixed.reshape(token_count, -1).astype(jnp.bfloat16)


def local(
    residual_input,
    new_token_queries,
    new_token_keys,
    new_token_values,
    key_page_pool,
    value_page_pool,
    request_page_table,
    page_token_length,
    request_token_length,
    request_adapter,
    adapter_table_row,
    output_weight,
    adapter_down_weight,
    adapter_up_weight,
    norm_scale_row,
):
    owners = lax.axis_size("req")
    groups = lax.axis_size("tp")
    requests_here = request_page_table.shape[0]
    page_rows = key_page_pool.shape[1]
    token_count = new_token_queries.shape[0]
    width_part = residual_input.shape[1]
    head_cols = key_page_pool.shape[2]
    down_cols = adapter_down_weight.shape[2]
    adapter_pair = jnp.concatenate([adapter_down_weight, adapter_up_weight], axis=2)
    adapters_everywhere = lax.all_gather(adapter_pair, "req", axis=0, tiled=True)
    wanted = lax.all_to_all(request_page_table, "req", split_axis=1, concat_axis=1, tiled=True)
    page_picks = jnp.maximum(wanted, 0)
    kv_pool = jnp.concatenate([key_page_pool, value_page_pool], axis=2)
    kv_out = kv_pool[page_picks]
    kv_back = lax.all_to_all(kv_out, "req", split_axis=1, concat_axis=1, tiled=True)
    kv_back = kv_back.reshape(requests_here, owners * page_rows, 2 * head_cols)
    gathered_keys = kv_back[:, :, :head_cols]
    gathered_values = kv_back[:, :, head_cols:]
    usable = (
        jnp.arange(page_rows, dtype=jnp.int32)[None, None, :] < page_token_length[:, :, None]
    ).reshape(requests_here, owners * page_rows)
    lengths = request_token_length[0]
    positions = jnp.arange(token_count, dtype=jnp.int32)
    ends = jnp.cumsum(lengths)
    owner_request = jnp.sum((positions[:, None] >= ends[None, :]).astype(jnp.int32), axis=1)
    attention = attend(
        new_token_queries,
        new_token_keys,
        new_token_values,
        gathered_keys,
        gathered_values,
        usable,
        owner_request,
    )
    adapters_all = adapter_table_row.shape[0]
    matches = request_adapter[0][:, None] == jnp.arange(adapters_all, dtype=jnp.int32)[None, :]
    chosen_pages = jnp.sum(jnp.where(matches, adapter_table_row[None, :], 0), axis=1)
    rows_here = adapters_everywhere.shape[0]
    picker = (chosen_pages[:, None] == jnp.arange(rows_here, dtype=jnp.int32)[None, :]).astype(
        jnp.bfloat16
    )
    selected = jnp.einsum(
        "rk,kab->rab", picker, adapters_everywhere, preferred_element_type=jnp.float32
    ).astype(jnp.bfloat16)
    adapter_in = selected[:, :, :down_cols]
    adapter_out = selected[:, :, down_cols:]
    rank_size = adapter_in.shape[1]
    selector = (
        owner_request[:, None] == jnp.arange(requests_here, dtype=jnp.int32)[None, :]
    ).astype(jnp.float32)
    selector_half = selector.astype(jnp.bfloat16)
    base_part = jnp.dot(attention, output_weight, preferred_element_type=jnp.float32)
    low_terms = jnp.einsum("tc,rkc->trk", attention, adapter_in, preferred_element_type=jnp.float32)
    low_part = jnp.sum(low_terms * selector[:, :, None], axis=1)
    base_slots = base_part.astype(jnp.bfloat16).reshape(token_count, groups, width_part)
    base_slots = jnp.transpose(base_slots, (1, 0, 2))
    low_slots = jnp.broadcast_to(
        low_part.astype(jnp.bfloat16)[None], (groups, token_count, rank_size)
    )
    pad_cols = -(width_part + rank_size) % 128
    slots = jnp.concatenate(
        [base_slots, low_slots, jnp.zeros((groups, token_count, pad_cols), jnp.bfloat16)], axis=2
    )
    arrived = lax.all_to_all(slots, "tp", split_axis=0, concat_axis=0, tiled=True)
    arrived = arrived.astype(jnp.float32)
    base_local = jnp.sum(arrived[:, :, :width_part], axis=0)
    low_sum = jnp.sum(arrived[:, :, width_part : width_part + rank_size], axis=0)
    rows_masked = (low_sum.astype(jnp.bfloat16)[:, None, :] * selector_half[:, :, None]).reshape(
        token_count, requests_here * rank_size
    )
    projected = base_local + adapter_scale * jnp.dot(
        rows_masked,
        adapter_out.reshape(requests_here * rank_size, width_part),
        preferred_element_type=jnp.float32,
    )
    square_part = jnp.sum(projected * projected, axis=1)
    square_sum = lax.psum(square_part, "tp")
    mean_square = square_sum / (groups * width_part)
    scaled = projected * lax.rsqrt(mean_square + epsilon)[:, None]
    return (residual_input.astype(jnp.float32) + scaled * norm_scale_row).astype(jnp.bfloat16)


def solution(mesh):
    in_specs = (
        P("req", "tp"),
        P("req", "tp"),
        P("req", "tp"),
        P("req", "tp"),
        P("req", None, "tp"),
        P("req", None, "tp"),
        P("req", None),
        P("req", None),
        P("req", None),
        P("req", None),
        P(),
        P("tp", None),
        P("req", None, "tp"),
        P("req", None, "tp"),
        P("tp"),
    )
    out_specs = P("req", "tp")
    return jax.shard_map(local, mesh=mesh, in_specs=in_specs, out_specs=out_specs, check_vma=False)
```

profile of v0, /device:TPU:8, one launch (start us, length us, event | category | flops | bytes accessed | tf_op | source)
XLA Modules:
  0.0 186.8 jit_solution(3870955451242989684)
XLA Ops:
  6.5 1.4 copy.88
  8.0 13.8 %all-to-all-start = ((s32[2,64,1]{0,2,1:T(1,128)}), s32[2,64,1]{0,2,1:T(1,128)S(1)}, u32[]{:S(2)}, u32[]{:S(2)}) async-start(s32[2,64,1]{0,2,1:T(1,128)} %copy.88), calls=%async_computation | async-start | bytes 65536 | tf_op jit(solution)/shard_map/all_to_all | solution.py:80
  21.8 1.4 pad_maximum_fusion.1
  23.2 1.1 pad_maximum_fusion
  24.2 7.0 %all-to-all-done = s32[2,64,1]{0,2,1:T(1,128)S(1)} async-done(((s32[2,64,1]{0,2,1:T(1,128)}), s32[2,64,1]{0,2,1:T(1,128)S(1)}, u32[]{:S(2)}, u32[]{:S(2)}) %all-to-all-start) | async-done | bytes 544 | tf_op jit(solution)/shard_map/all_to_all | solution.py:80
  31.4 0.7 gather_fusion
  32.1 1.6 copy.90
  33.7 4.8 %all-to-all-start.1 = ((bf16[2,64,16,512]{3,2,0,1:T(8,128)(2,1)}), bf16[2,64,16,512]{3,2,0,1:T(8,128)(2,1)S(1)}, u32[]{:S(2)}, u32[]{:S(2)}) async-start(bf16[2,64,16,512]{3,2,0,1:T(8,128)(2,1)} %copy.90), calls=%async_computation.1 | async-start | bytes 4194304 | tf_op jit(solution)/shard_map/all_to_all | solution.py:84
  38.5 0.7 copy.92
  39.9 0.2 fusion.31
  40.2 0.3 broadcast_and_fusion
  40.6 0.9 fusion.38
  41.4 71.5 %all-gather.2.cloned.1.call-done = bf16[64,16,960]{2,1,0:T(8,128)(2,1)} async-done(((bf16[1,16,960]{2,1,0:T(8,128)(2,1)}), bf16[64,16,960]{2,1,0:T(8,128)(2,1)}) %all-gather.2.cloned.1.call-update) | async-done | bytes 1966096 | tf_op jit(solution)/shard_map/all_gather | solution.py:79
  112.9 3.9 %fusion.10 = bf16[2,16,960]{2,0,1:T(2,128)(2,1)S(1)} fusion(bf16[64,16,960]{2,1,0:T(8,128)(2,1)} %all-gather.2.cloned.1.call-done, s32[2]{0:T(128)S(1)} %fusion.31), kind=kOutput, calls=%fused_computation.19 | convolution fusion | flops 3963008 | bytes 2027528 | tf_op jit(solution)/shard_map/rk,kab->rab/dot_general | solution.py:111
  116.8 0.2 copy.91
  117.0 0.4 copy-done.5
  117.4 1.3 copy-done.1
  118.9 1.4 copy.93
  120.3 0.5 copy-done.2
  120.8 1.4 fusion.37
  122.5 0.7 copy-done.6
  123.2 0.3 fusion.3
  123.7 0.6 convolution_convert_fusion.1
  124.2 1.5 copy-done.3
  125.7 0.7 convolution_convert_fusion
  126.4 0.6 copy.99
  127.2 1.3 maximum_maximum_fusion
  128.4 6.8 %all-to-all-start.2 = ((bf16[8,128,512]{1,2,0:T(8,128)(2,1)}), bf16[8,128,512]{1,2,0:T(8,128)(2,1)S(1)}, u32[]{:S(2)}, u32[]{:S(2)}) async-start(bf16[8,128,512]{1,2,0:T(8,128)(2,1)} %maximum_maximum_fusion), calls=%async_computation.2 | async-start | bytes 2097152 | tf_op jit(solution)/shard_map/all_to_all | solution.py:133
  135.3 27.7 %all-to-all-done.2 = bf16[8,128,512]{1,2,0:T(8,128)(2,1)S(1)} async-done(((bf16[8,128,512]{1,2,0:T(8,128)(2,1)}), bf16[8,128,512]{1,2,0:T(8,128)(2,1)S(1)}, u32[]{:S(2)}, u32[]{:S(2)}) %all-to-all-start.2) | async-done | bytes 1048608 | tf_op jit(solution)/shard_map/all_to_all | solution.py:133
  163.2 0.3 multiply_reduce_fusion
  163.5 15.6 %psum.7 = f32[128]{0:T(128)S(1)} all-reduce(f32[128]{0:T(128)S(1)} %get-tuple-element.12), channel_id=1, replica_groups=mesh['req'=64,'tp'=8] {'tp'}, use_global_device_ids=true, to_apply=%region_10.11 | all-reduce | flops 128 | bytes 1024 | tf_op jit(solution)/shard_map/psum | solution.py:146
  179.1 0.8 add_convert_fusion
  (58 shorter events, 1.8 us)
Async XLA Ops:
  6.5 34.0 %copy-start = (bf16[128,256]{1,0:T(8,128)(2,1)S(1)}, bf16[128,256]{1,0:T(8,128)(2,1)}, u32[]{:S(2)}) copy-start(bf16[128,256]{1,0:T(8,128)(2,1)} %param.17) | copy-start | bytes 196612
  8.0 23.2 %all-to-all-start = ((s32[2,64,1]{0,2,1:T(1,128)}), s32[2,64,1]{0,2,1:T(1,128)S(1)}, u32[]{:S(2)}, u32[]{:S(2)}) async-start(s32[2,64,1]{0,2,1:T(1,128)} %copy.88), calls=%async_computation | async-start | bytes 65536 | tf_op jit(solution)/shard_map/all_to_all | solution.py:80
  21.7 91.2 %all-gather.2.cloned.1.call-start = ((), (), s32[]{:S(2)}) async-start(), calls=%async_computation.3 | async-start | bytes 2129920 | tf_op jit(solution)/shard_map/all_gather | solution.py:79
  33.7 4.9 %copy-start.8 = (bf16[128,256]{1,0:T(8,128)(2,1)S(1)}, bf16[128,256]{1,0:T(8,128)(2,1)}, u32[]{:S(2)}) copy-start(bf16[128,256]{1,0:T(8,128)(2,1)} %param.18) | copy-start | bytes 196612
  33.7 5.6 %copy-start.11 = (s32[2,64]{1,0:T(2,128)S(1)}, s32[2,64]{1,0:T(2,128)}, u32[]{:S(2)}) copy-start(s32[2,64]{1,0:T(2,128)} %param.22) | copy-start | bytes 1540
  33.7 5.9 %copy-start.13 = (s32[1,2]{1,0:T(1,128)S(1)}, s32[1,2]{1,0:T(1,128)}, u32[]{:S(2)}) copy-start(s32[1,2]{1,0:T(1,128)} %param.23) | copy-start | bytes 28
  33.7 6.2 %copy-start.14 = (s32[64]{0:T(128)S(1)}, s32[64]{0:T(128)}, u32[]{:S(2)}) copy-start(s32[64]{0:T(128)} %param.25) | copy-start | bytes 772
  33.7 6.2 %copy-start.15 = (s32[1,2]{1,0:T(1,128)S(1)}, s32[1,2]{1,0:T(1,128)}, u32[]{:S(2)}) copy-start(s32[1,2]{1,0:T(1,128)} %param.24) | copy-start | bytes 28
  33.7 6.9 %copy-start.12 = (bf16[128,512]{1,0:T(8,128)(2,1)S(1)}, bf16[128,512]{1,0:T(8,128)(2,1)}, u32[]{:S(2)}) copy-start(bf16[128,512]{1,0:T(8,128)(2,1)} %param.16) | copy-start | bytes 393220
  33.7 83.1 %all-to-all-start.1 = ((bf16[2,64,16,512]{3,2,0,1:T(8,128)(2,1)}), bf16[2,64,16,512]{3,2,0,1:T(8,128)(2,1)S(1)}, u32[]{:S(2)}, u32[]{:S(2)}) async-start(bf16[2,64,16,512]{3,2,0,1:T(8,128)(2,1)} %copy.90), calls=%async_computation.1 | async-start | bytes 4194304 | tf_op jit(solution)/shard_map/all_to_all | solution.py:84
  116.8 0.6 copy-start.5
  117.4 1.3 copy-start.1
  118.8 2.0 %copy-start.2 = (bf16[2,64,16,512]{3,2,1,0:T(8,128)(2,1)S(1)}, bf16[2,64,16,512]{3,2,1,0:T(8,128)(2,1)}, u32[]{:S(2)}) copy-start(bf16[2,64,16,512]{3,2,1,0:T(8,128)(2,1)} %copy-done.1) | copy-start | bytes 6291460
  122.3 0.9 copy-start.6
  122.4 1.2 copy-start.4
  122.4 1.2 copy-start.9
  123.7 2.0 %copy-start.3 = (bf16[512,3584]{1,0:T(8,128)(2,1)S(1)}, bf16[512,3584]{1,0:T(8,128)(2,1)}, u32[]{:S(2)}) copy-start(bf16[512,3584]{1,0:T(8,128)(2,1)} %param.26) | copy-start | bytes 11010052
  125.7 1.3 slice-start
  128.4 34.5 %all-to-all-start.2 = ((bf16[8,128,512]{1,2,0:T(8,128)(2,1)}), bf16[8,128,512]{1,2,0:T(8,128)(2,1)S(1)}, u32[]{:S(2)}, u32[]{:S(2)}) async-start(bf16[8,128,512]{1,2,0:T(8,128)(2,1)} %maximum_maximum_fusion), calls=%async_computation.2 | async-start | bytes 2097152 | tf_op jit(solution)/shard_map/all_to_all | solution.py:133
  135.3 27.9 %slice-start.1 = ((bf16[2,16,960]{2,0,1:T(2,128)(2,1)}), bf16[2,16,448]{2,0,1:T(2,128)(2,1)S(1)}, s32[]{:S(2)}) async-start(bf16[2,16,960]{2,0,1:T(2,128)(2,1)} %copy-done.5), calls=%async_computation.5 | async-start | bytes 65536 | tf_op jit(solution)/shard_map/slice | solution.py:115
  163.1 16.1 %copy-start.7 = (bf16[128,448]{0,1:T(8,128)(2,1)S(1)}, bf16[128,448]{0,1:T(8,128)(2,1)}, u32[]{:S(2)}) copy-start(bf16[128,448]{0,1:T(8,128)(2,1)} %param.15) | copy-start | bytes 344068
  163.1 16.1 %copy-start.10 = (f32[448]{0:T(512)S(1)}, f32[448]{0:T(512)}, u32[]{:S(2)}) copy-start(f32[448]{0:T(512)} %param.29) | copy-start | bytes 5380
Sparse Core Ops, SparseCore 0:
  25.9 86.9 all-gather.1
where the time goes:
time: 187 us
  waiting for transfers between devices  106 us (57%)
  starting transfers between devices  25.5 us (14%)
  blocking collectives  15.6 us (8%)
  between operations  13.7 us (7%)
  local copies, waits for them, and re-layouts  12.1 us (6%)
  matrix products  7.86 us (4%)
  other arithmetic  5.9 us (3%)
    all_gather x1, waiting for transfers between devices, local(): lax.all_gather(adapter_pair, 'req', axis=0, tiled=True)  71.5 us
    all_to_all x1, waiting for transfers between devices, local(): lax.all_to_all(slots, 'tp', split_axis=0, concat_axis=0, tiled=True)  27.7 us
    psum x1, blocking collectives, local(): square_sum = lax.psum(square_part, 'tp')  15.6 us
    all_to_all x1, starting transfers between devices, local(): lax.all_to_all(request_page_table, 'req', split_axis=1, concat_axis=1, ti...  13.8 us
    all_to_all x1, waiting for transfers between devices, local(): lax.all_to_all(request_page_table, 'req', split_axis=1, concat_axis=1, ti...  6.97 us
    all_to_all x1, starting transfers between devices, local(): lax.all_to_all(slots, 'tp', split_axis=0, concat_axis=0, tiled=True)  6.83 us
    unnamed x33, local copies, waits for them, and re-layouts  5.44 us
    all_to_all x1, starting transfers between devices, local(): lax.all_to_all(kv_out, 'req', split_axis=1, concat_axis=1, tiled=True)  4.84 us
  transfers between devices with their start and end apart: 4, of which 3 were waited for; matrix products, arithmetic and copies ran while one was open for 6% of the time, Pallas kernels for 0%

commit v1 on v0

--- a/solution.py
+++ b/solution.py
@@ -2,6 +2,7 @@
 import jax.numpy as jnp
 from jax import lax
 from jax.sharding import PartitionSpec as P
+from jax.lax import all_to_all, axis_size
 
 HEAD_SIZE = 256
 epsilon = 1e-06
@@ -76,7 +77,15 @@
     head_cols = key_page_pool.shape[2]
     down_cols = adapter_down_weight.shape[2]
     adapter_pair = jnp.concatenate([adapter_down_weight, adapter_up_weight], axis=2)
-    adapters_everywhere = lax.all_gather(adapter_pair, "req", axis=0, tiled=True)
+    adapters_everywhere = jnp.concatenate(
+        all_to_all(
+            jnp.stack([adapter_pair] * axis_size("req")),
+            axis_name="req",
+            split_axis=0,
+            concat_axis=0,
+        ),
+        axis=0,
+    )
     wanted = lax.all_to_all(request_page_table, "req", split_axis=1, concat_axis=1, tiled=True)
     page_picks = jnp.maximum(wanted, 0)
     kv_pool = jnp.concatenate([key_page_pool, value_page_pool], axis=2)

time: 187 us -> 204 us (1.091)
  waiting for transfers between devices: 106 us -> 129 us
  between operations: 13.7 us -> 0.32 us
  starting transfers between devices: 25.5 us -> 32.9 us
    all_gather x1 -> x0, waiting for transfers between devices: 71.5 us -> none  [local(): lax.all_gather(adapter_pair, 'req', axis=0, tiled=True)]
    all_to_all x0 -> x1, waiting for transfers between devices: none -> 48.4 us  [local(): all_to_all(jnp.stack([adapter_pair] * axis_size('req')), axis_name='req',...]
    all_to_all x1, waiting for transfers between devices: 0.01 us -> 44.4 us  [local(): lax.all_to_all(kv_out, 'req', split_axis=1, concat_axis=1, tiled=True)]
    all_to_all x0 -> x1, starting transfers between devices: none -> 5.7 us  [local(): all_to_all(jnp.stack([adapter_pair] * axis_size('req')), axis_name='req',...]
    unnamed x33 -> x37, local copies, waits for them, and re-layouts: 5.44 us -> 5.01 us
  transfers between devices with their start and end apart: 4 -> 4, of which waited for: 3 -> 4; matrix products, arithmetic and copies ran while one was open for 6% -> 5% of each run, Pallas kernels for 0% -> 0%
where the time goes in v1:
time: 204 us; the launch traced here: 203 us
  waiting for transfers between devices  129 us (63%)
  starting transfers between devices  32.9 us (16%)
  blocking collectives  15.6 us (8%)
  local copies, waits for them, and re-layouts  13.2 us (6%)
  matrix products  7.84 us (4%)
  other arithmetic  4.26 us (2%)
    all_to_all x1, waiting for transfers between devices, local(): all_to_all(jnp.stack([adapter_pair] * axis_size('req')), axis_name='req',...  48.4 us
    all_to_all x1, waiting for transfers between devices, local(): lax.all_to_all(kv_out, 'req', split_axis=1, concat_axis=1, tiled=True)  44.4 us
    all_to_all x1, waiting for transfers between devices, local(): lax.all_to_all(slots, 'tp', split_axis=0, concat_axis=0, tiled=True)  27.5 us
    psum x1, blocking collectives, local(): square_sum = lax.psum(square_part, 'tp')  15.6 us
    all_to_all x1, starting transfers between devices, local(): lax.all_to_all(request_page_table, 'req', split_axis=1, concat_axis=1, ti...  13.8 us
    all_to_all x1, waiting for transfers between devices, local(): lax.all_to_all(request_page_table, 'req', split_axis=1, concat_axis=1, ti...  8.71 us
    all_to_all x1, starting transfers between devices, local(): lax.all_to_all(slots, 'tp', split_axis=0, concat_axis=0, tiled=True)  7.56 us
    all_to_all x1, starting transfers between devices, local(): lax.all_to_all(kv_out, 'req', split_axis=1, concat_axis=1, tiled=True)  5.89 us
  transfers between devices with their start and end apart: 4, of which 4 were waited for; matrix products, arithmetic and copies ran while one was open for 5% of the time, Pallas kernels for 0%

profile of v1, /device:TPU:8, one launch (start us, length us, event | category | flops | bytes accessed | tf_op | source)
XLA Modules:
  0.0 203.3 jit_solution(11416308881236625925)
XLA Ops:
  0.0 1.4 copy.84
  1.4 13.8 %all-to-all-start = ((s32[2,64,1]{0,2,1:T(1,128)}), s32[2,64,1]{0,2,1:T(1,128)S(1)}, u32[]{:S(2)}, u32[]{:S(2)}) async-start(s32[2,64,1]{0,2,1:T(1,128)} %copy.84), calls=%async_computation | async-start | bytes 65536 | tf_op jit(solution)/shard_map/all_to_all | solution.py:89
  15.2 0.7 maximum_bitcast_fusion.2
  16.0 8.7 %all-to-all-done = s32[2,64,1]{0,2,1:T(1,128)S(1)} async-done(((s32[2,64,1]{0,2,1:T(1,128)}), s32[2,64,1]{0,2,1:T(1,128)S(1)}, u32[]{:S(2)}, u32[]{:S(2)}) %all-to-all-start) | async-done | bytes 544 | tf_op jit(solution)/shard_map/all_to_all | solution.py:89
  24.7 1.6 stack.2
  26.2 5.7 %all-to-all-start.2 = ((bf16[64,1,16,960]{3,2,1,0:T(8,128)(2,1)}), bf16[64,1,16,960]{3,2,1,0:T(8,128)(2,1)}, u32[]{:S(2)}, u32[]{:S(2)}) async-start(bf16[64,1,16,960]{3,2,1,0:T(8,128)(2,1)} %stack.2), calls=%async_computation.2 | async-start | bytes 4194304 | tf_op jit(solution)/shard_map/all_to_all | solution.py:81
  32.2 0.7 gather_fusion
  32.9 1.6 copy.86
  34.5 48.4 %all-to-all-done.2 = bf16[64,1,16,960]{3,2,1,0:T(8,128)(2,1)} async-done(((bf16[64,1,16,960]{3,2,1,0:T(8,128)(2,1)}), bf16[64,1,16,960]{3,2,1,0:T(8,128)(2,1)}, u32[]{:S(2)}, u32[]{:S(2)}) %all-to-all-start.2) | async-done | bytes 1966112 | tf_op jit(solution)/shard_map/all_to_all | solution.py:81
  82.9 5.9 %all-to-all-start.1 = ((bf16[2,64,16,512]{3,2,0,1:T(8,128)(2,1)}), bf16[2,64,16,512]{3,2,0,1:T(8,128)(2,1)S(1)}, u32[]{:S(2)}, u32[]{:S(2)}) async-start(bf16[2,64,16,512]{3,2,0,1:T(8,128)(2,1)} %copy.86), calls=%async_computation.1 | async-start | bytes 4194304 | tf_op jit(solution)/shard_map/all_to_all | solution.py:93
  88.8 0.7 copy.88
  90.2 0.2 fusion.32
  90.5 0.3 broadcast_and_fusion
  90.9 0.8 fusion.39
  91.7 3.9 %fusion.11 = bf16[2,16,960]{2,0,1:T(2,128)(2,1)S(1)} fusion(bf16[64,1,16,960]{3,2,1,0:T(8,128)(2,1)} %all-to-all-done.2, s32[2]{0:T(128)S(1)} %fusion.32), kind=kOutput, calls=%fused_computation.20 | convolution fusion | flops 3963008 | bytes 2027528 | tf_op jit(solution)/shard_map/rk,kab->rab/dot_general | solution.py:120
  95.6 44.4 %all-to-all-done.1 = bf16[2,64,16,512]{3,2,0,1:T(8,128)(2,1)S(1)} async-done(((bf16[2,64,16,512]{3,2,0,1:T(8,128)(2,1)}), bf16[2,64,16,512]{3,2,0,1:T(8,128)(2,1)S(1)}, u32[]{:S(2)}, u32[]{:S(2)}) %all-to-all-start.1) | async-done | bytes 2097184 | tf_op jit(solution)/shard_map/all_to_all | solution.py:93
  140.2 1.3 copy-done.1
  141.6 1.4 copy.89
  143.0 0.5 copy-done.2
  143.6 1.4 fusion.38
  145.2 0.7 copy-done.8
  145.9 0.3 fusion.3
  146.4 0.6 convolution_convert_fusion.1
  147.0 1.5 copy-done.3
  148.5 0.7 convolution_convert_fusion
  149.1 0.6 copy.95
  149.9 1.3 maximum_maximum_fusion
  151.2 7.6 %all-to-all-start.3 = ((bf16[8,128,512]{1,2,0:T(8,128)(2,1)}), bf16[8,128,512]{1,2,0:T(8,128)(2,1)S(1)}, u32[]{:S(2)}, u32[]{:S(2)}) async-start(bf16[8,128,512]{1,2,0:T(8,128)(2,1)} %maximum_maximum_fusion), calls=%async_computation.3 | async-start | bytes 2097152 | tf_op jit(solution)/shard_map/all_to_all | solution.py:142
  158.7 27.5 %all-to-all-done.3 = bf16[8,128,512]{1,2,0:T(8,128)(2,1)S(1)} async-done(((bf16[8,128,512]{1,2,0:T(8,128)(2,1)}), bf16[8,128,512]{1,2,0:T(8,128)(2,1)S(1)}, u32[]{:S(2)}, u32[]{:S(2)}) %all-to-all-start.3) | async-done | bytes 1048608 | tf_op jit(solution)/shard_map/all_to_all | solution.py:142
  186.6 0.3 multiply_reduce_fusion
  186.8 15.6 %psum.7 = f32[128]{0:T(128)S(1)} all-reduce(f32[128]{0:T(128)S(1)} %get-tuple-element.12), channel_id=1, replica_groups=mesh['req'=64,'tp'=8] {'tp'}, use_global_device_ids=true, to_apply=%region_10.11 | all-reduce | flops 128 | bytes 1024 | tf_op jit(solution)/shard_map/psum | solution.py:155
  202.5 0.8 add_convert_fusion
  (62 shorter events, 1.9 us)
Async XLA Ops:
  0.0 90.9 %copy-start = (bf16[128,256]{1,0:T(8,128)(2,1)S(1)}, bf16[128,256]{1,0:T(8,128)(2,1)}, u32[]{:S(2)}) copy-start(bf16[128,256]{1,0:T(8,128)(2,1)} %param.17) | copy-start | bytes 196612
  1.4 23.2 %all-to-all-start = ((s32[2,64,1]{0,2,1:T(1,128)}), s32[2,64,1]{0,2,1:T(1,128)S(1)}, u32[]{:S(2)}, u32[]{:S(2)}) async-start(s32[2,64,1]{0,2,1:T(1,128)} %copy.84), calls=%async_computation | async-start | bytes 65536 | tf_op jit(solution)/shard_map/all_to_all | solution.py:89
  26.2 5.7 %copy-start.6 = (bf16[24,16,256]{2,1,0:T(8,128)(2,1)S(1)}, bf16[24,16,256]{2,1,0:T(8,128)(2,1)}, u32[]{:S(2)}) copy-start(bf16[24,16,256]{2,1,0:T(8,128)(2,1)} %param.20) | copy-start | bytes 589828
  26.2 5.7 %copy-start.7 = (bf16[24,16,256]{2,1,0:T(8,128)(2,1)S(1)}, bf16[24,16,256]{2,1,0:T(8,128)(2,1)}, u32[]{:S(2)}) copy-start(bf16[24,16,256]{2,1,0:T(8,128)(2,1)} %param.19) | copy-start | bytes 589828
  26.2 56.7 %all-to-all-start.2 = ((bf16[64,1,16,960]{3,2,1,0:T(8,128)(2,1)}), bf16[64,1,16,960]{3,2,1,0:T(8,128)(2,1)}, u32[]{:S(2)}, u32[]{:S(2)}) async-start(bf16[64,1,16,960]{3,2,1,0:T(8,128)(2,1)} %stack.2), calls=%async_computation.2 | async-start | bytes 4194304 | tf_op jit(solution)/shard_map/all_to_all | solution.py:81
  34.5 54.4 %copy-start.10 = (bf16[128,256]{1,0:T(8,128)(2,1)S(1)}, bf16[128,256]{1,0:T(8,128)(2,1)}, u32[]{:S(2)}) copy-start(bf16[128,256]{1,0:T(8,128)(2,1)} %param.18) | copy-start | bytes 196612
  34.5 55.1 %copy-start.13 = (s32[2,64]{1,0:T(2,128)S(1)}, s32[2,64]{1,0:T(2,128)}, u32[]{:S(2)}) copy-start(s32[2,64]{1,0:T(2,128)} %param.22) | copy-start | bytes 1540
  34.5 55.4 %copy-start.15 = (s32[1,2]{1,0:T(1,128)S(1)}, s32[1,2]{1,0:T(1,128)}, u32[]{:S(2)}) copy-start(s32[1,2]{1,0:T(1,128)} %param.23) | copy-start | bytes 28
  34.5 55.7 %copy-start.16 = (s32[64]{0:T(128)S(1)}, s32[64]{0:T(128)}, u32[]{:S(2)}) copy-start(s32[64]{0:T(128)} %param.25) | copy-start | bytes 772
  34.5 55.7 %copy-start.17 = (s32[1,2]{1,0:T(1,128)S(1)}, s32[1,2]{1,0:T(1,128)}, u32[]{:S(2)}) copy-start(s32[1,2]{1,0:T(1,128)} %param.24) | copy-start | bytes 28
  34.5 56.4 %copy-start.14 = (bf16[128,512]{1,0:T(8,128)(2,1)S(1)}, bf16[128,512]{1,0:T(8,128)(2,1)}, u32[]{:S(2)}) copy-start(bf16[128,512]{1,0:T(8,128)(2,1)} %param.16) | copy-start | bytes 393220
  82.9 57.0 %all-to-all-start.1 = ((bf16[2,64,16,512]{3,2,0,1:T(8,128)(2,1)}), bf16[2,64,16,512]{3,2,0,1:T(8,128)(2,1)S(1)}, u32[]{:S(2)}, u32[]{:S(2)}) async-start(bf16[2,64,16,512]{3,2,0,1:T(8,128)(2,1)} %copy.86), calls=%async_computation.1 | async-start | bytes 4194304 | tf_op jit(solution)/shard_map/all_to_all | solution.py:93
  95.6 44.6 %copy-start.5 = (bf16[2,16,960]{2,0,1:T(2,128)(2,1)}, bf16[2,16,960]{2,0,1:T(2,128)(2,1)S(1)}, u32[]{:S(2)}) copy-start(bf16[2,16,960]{2,0,1:T(2,128)(2,1)S(1)} %fusion.11) | copy-start | bytes 184324
  140.2 1.3 copy-start.1
  141.6 2.0 copy-start.2
  145.0 0.9 copy-start.8
  145.2 1.2 copy-start.4
  145.2 1.2 copy-start.11
  146.4 2.0 %copy-start.3 = (bf16[512,3584]{1,0:T(8,128)(2,1)S(1)}, bf16[512,3584]{1,0:T(8,128)(2,1)}, u32[]{:S(2)}) copy-start(bf16[512,3584]{1,0:T(8,128)(2,1)} %param.26) | copy-start | bytes 11010052
  148.4 1.3 slice-start
  151.2 35.1 %all-to-all-start.3 = ((bf16[8,128,512]{1,2,0:T(8,128)(2,1)}), bf16[8,128,512]{1,2,0:T(8,128)(2,1)S(1)}, u32[]{:S(2)}, u32[]{:S(2)}) async-start(bf16[8,128,512]{1,2,0:T(8,128)(2,1)} %maximum_maximum_fusion), calls=%async_computation.3 | async-start | bytes 2097152 | tf_op jit(solution)/shard_map/all_to_all | solution.py:142
  158.7 27.8 %slice-start.1 = ((bf16[2,16,960]{2,0,1:T(2,128)(2,1)}), bf16[2,16,448]{2,0,1:T(2,128)(2,1)S(1)}, s32[]{:S(2)}) async-start(bf16[2,16,960]{2,0,1:T(2,128)(2,1)} %copy-done.5), calls=%async_computation.5 | async-start | bytes 65536 | tf_op jit(solution)/shard_map/slice | solution.py:124
  186.4 16.1 %copy-start.9 = (bf16[128,448]{0,1:T(8,128)(2,1)S(1)}, bf16[128,448]{0,1:T(8,128)(2,1)}, u32[]{:S(2)}) copy-start(bf16[128,448]{0,1:T(8,128)(2,1)} %param.15) | copy-start | bytes 344068
  186.4 16.1 %copy-start.12 = (f32[448]{0:T(512)S(1)}, f32[448]{0:T(512)}, u32[]{:S(2)}) copy-start(f32[448]{0:T(512)} %param.29) | copy-start | bytes 5380
